TPU v7x, 256 devices: a whole 4x4x8 slice. The times are simulated.
256 devices in a mesh: seq: 64 (over z, y, core), tensor: 4 (over x).
Axes of the slice: x: 4, y: 4, z: 8, core: 2. Of those that a mesh axis runs over, the one named last changes fastest.
Arguments:
- new_states: bfloat16 [4, 128, 1024], P(None, None, 'tensor'), may hold values from -6 to 6
- self_query: bfloat16 [1024, 1024], P(None, 'tensor'), may hold values from -0.1875 to 0.1875
- self_key: bfloat16 [1024, 1024], P(None, 'tensor'), may hold values from -0.375 to 0.375
- self_value: bfloat16 [1024, 1024], P(None, 'tensor'), may hold values from -0.1875 to 0.1875
- self_output: bfloat16 [1024, 1024], P('tensor'), may hold values from -0.1875 to 0.1875
- cross_query: bfloat16 [1024, 1024], P(None, 'tensor'), may hold values from -0.1875 to 0.1875
- cross_output: bfloat16 [1024, 1024], P('tensor'), may hold values from -0.1875 to 0.1875
- feed_up: bfloat16 [1024, 4096], P(None, 'tensor'), may hold values from -0.1875 to 0.1875
- feed_down: bfloat16 [4096, 1024], P('tensor'), may hold values from -0.09375 to 0.09375
- norm_self: float32 [1024], replicated, may hold values from 0.25 to 1.75
- norm_cross: float32 [1024], replicated, may hold values from 0.25 to 1.75
- norm_feed: float32 [1024], replicated, may hold values from 0.25 to 1.75
- self_cache: bfloat16 [1536, 2, 128, 1024], P('seq', None, None, 'tensor'), may hold values from -240 to 240
- cross_cache: bfloat16 [128, 2, 512, 1024], P(None, None, 'seq', 'tensor'), may hold values from -240 to 240
- cache_lengths: int32 [128], replicated, may hold values from 1 to 16384, as said below
- page_table: int32 [128, 128], replicated, may hold values from -1 to 1535, as said below
- request_order: int32 [128], replicated, may hold values from 0 to 127, each once
- encoder_lengths: int32 [128], replicated, may hold values from 1 to 512, as said below
Outputs:
- out: bfloat16 [4, 128, 1024], P(None, None, 'tensor')
Inputs may be any that keep to these rules, and one draw needn't show every extreme that they name: `cache_lengths`: one request has exactly 16384 cached tokens. `page_table`: row r holds the slots of request r's pages in order: its first ceil(cache_lengths[r] / 128) entries are slots, page p holding positions p * 128 to (p + 1) * 128 - 1, and no slot appears twice in the table; the other entries are -1. Slot s belongs to seq index s // 24. `encoder_lengths`: one request has exactly 512 encoder positions.
All inputs are finite; a program needn't handle non-finite values.
Results may differ from a plain program's by a relative error of at most 0.014.
The roundings to bfloat16 on the way count: a program that leaves them out, or rounds other values in their place, can miss the bound.
Values may be sent and summed in bfloat16 or wider, within the bound.
No kernel may reach another device: no remote copies, remote signals or barrier semaphores. Data moves between devices by JAX's collectives and lax.ppermute only.
A program may use at most 64 MiB of HBM per device.

v0:
```python
import jax
import jax.numpy as jnp
from jax import lax
from jax.sharding import PartitionSpec as P

HEAD_DIM = 64
EPSILON = 1e-05
NEG_FILL = -1e30


def layer_norm(summed, gain):
    center = jnp.mean(summed, axis=-1, keepdims=True)
    spread = jnp.mean(summed * summed, axis=-1, keepdims=True) - center * center
    return (summed - center) * lax.rsqrt(spread + EPSILON) * gain


def global_max(local_max):
    return lax.pmax(local_max, "seq")


def global_totals(denom, numer):
    return lax.psum((denom, numer), "seq")


def reduce_norm(residual, partial_value, gain):
    width = residual.shape[1]
    total = lax.psum(partial_value, "tensor")
    full = layer_norm(residual.astype(jnp.float32) + total, gain).astype(jnp.bfloat16)
    columns = width // lax.axis_size("tensor")
    return (full, lax.dynamic_slice_in_dim(full, lax.axis_index("tensor") * columns, columns, 1))


def on_device(
    new_states,
    self_query,
    self_key,
    self_value,
    self_output,
    cross_query,
    cross_output,
    feed_up,
    feed_down,
    norm_self,
    norm_cross,
    norm_feed,
    self_cache,
    cross_cache,
    cache_lengths,
    page_table,
    request_order,
    encoder_lengths,
):
    states = lax.all_gather(new_states, "tensor", axis=2, tiled=True)
    steps, requests, width = states.shape
    flat = states.reshape(steps * requests, width)
    local_width = self_query.shape[1]
    local_heads = local_width // HEAD_DIM
    scaling = HEAD_DIM ** (-0.5)
    queries = (jnp.dot(flat, self_query, preferred_element_type=jnp.float32) * scaling).astype(
        jnp.bfloat16
    )
    new_keys = jnp.dot(flat, self_key, preferred_element_type=jnp.float32).astype(jnp.bfloat16)
    new_values = jnp.dot(flat, self_value, preferred_element_type=jnp.float32).astype(jnp.bfloat16)
    query_grid = queries.reshape(steps, requests, local_heads, HEAD_DIM)
    key_grid = new_keys.reshape(steps, requests, local_heads, HEAD_DIM)
    value_grid = new_values.reshape(steps, requests, local_heads, HEAD_DIM)
    slot_count = self_cache.shape[0]
    page_width = self_cache.shape[2]
    max_pages = page_table.shape[1]
    seq_index = lax.axis_index("seq")
    flat_table = page_table.reshape(-1)
    entry_ids = jnp.arange(requests * max_pages, dtype=jnp.int32)
    entry_request = entry_ids // max_pages
    entry_page = entry_ids % max_pages
    slot_ids = seq_index * slot_count + jnp.arange(slot_count, dtype=jnp.int32)
    matches = flat_table[None, :] == slot_ids[:, None]
    slot_live = jnp.any(matches, axis=1)
    slot_owner = jnp.sum(jnp.where(matches, entry_request[None, :], 0), axis=1)
    slot_page = jnp.sum(jnp.where(matches, entry_page[None, :], 0), axis=1)
    request_ids = jnp.arange(requests, dtype=jnp.int32)
    slot_length = jnp.sum(
        jnp.where(slot_owner[:, None] == request_ids[None, :], cache_lengths[None, :], 0), axis=1
    )
    positions = slot_page[:, None] * page_width + jnp.arange(page_width, dtype=jnp.int32)[None, :]
    slot_valid = slot_live[:, None] & (positions < slot_length[:, None])
    slot_rows = slot_live[:, None] & (request_order[None, :] == slot_owner[:, None])
    rows_half = slot_rows.astype(jnp.bfloat16)
    rows_wide = slot_rows.astype(jnp.float32)
    slot_query = jnp.einsum(
        "pb,sbc->psc",
        rows_half,
        queries.reshape(steps, requests, local_width),
        preferred_element_type=jnp.float32,
    ).astype(jnp.bfloat16)
    slot_query = slot_query.reshape(slot_count, steps, local_heads, HEAD_DIM)
    cache_keys = self_cache[:, 0].reshape(slot_count, page_width, local_heads, HEAD_DIM)
    cache_values = self_cache[:, 1].reshape(slot_count, page_width, local_heads, HEAD_DIM)
    cache_scores = jnp.einsum(
        "pshd,pkhd->pshk", slot_query, cache_keys, preferred_element_type=jnp.float32
    )
    valid_grid = slot_valid[:, None, None, :]
    slot_max = jnp.max(jnp.where(valid_grid, cache_scores, NEG_FILL), axis=3)
    row_max = jnp.max(
        jnp.where(slot_rows[:, None, :, None], slot_max[:, :, None, :], NEG_FILL), axis=0
    )
    causal = jnp.arange(steps)[None, :] <= jnp.arange(steps)[:, None]
    new_scores = jnp.einsum(
        "tbhd,ubhd->bhtu", query_grid, key_grid, preferred_element_type=jnp.float32
    )
    new_scores = jnp.where(causal, new_scores, NEG_FILL)
    new_max = jnp.transpose(jnp.max(new_scores, axis=3), (2, 0, 1))
    top = global_max(jnp.maximum(row_max, new_max))
    slot_top = jnp.einsum("pb,sbh->psh", rows_wide, top, precision=lax.Precision.HIGHEST)
    cache_weights = jnp.exp(jnp.where(valid_grid, cache_scores - slot_top[..., None], NEG_FILL))
    cache_denom = jnp.sum(cache_weights, axis=3)
    cache_numer = jnp.einsum(
        "pshk,pkhd->pshd",
        cache_weights.astype(jnp.bfloat16),
        cache_values,
        preferred_element_type=jnp.float32,
    )
    row_denom = jnp.einsum("pb,psh->sbh", rows_wide, cache_denom, precision=lax.Precision.HIGHEST)
    row_numer = jnp.einsum("pb,pshd->sbhd", rows_wide, cache_numer, precision=lax.Precision.HIGHEST)
    total_denom, total_numer = global_totals(row_denom, row_numer)
    top_new = jnp.transpose(top, (1, 2, 0))[..., None]
    new_weights = jnp.where(causal, jnp.exp(new_scores - top_new), 0.0)
    new_denom = jnp.transpose(jnp.sum(new_weights, axis=3), (2, 0, 1))
    new_numer = jnp.einsum(
        "bhtu,ubhd->tbhd",
        new_weights.astype(jnp.bfloat16),
        value_grid,
        preferred_element_type=jnp.float32,
    )
    self_attn = ((total_numer + new_numer) / (total_denom + new_denom)[..., None]).astype(
        jnp.bfloat16
    )
    partial_value = jnp.dot(
        self_attn.reshape(steps * requests, local_width),
        self_output,
        preferred_element_type=jnp.float32,
    )
    first_full, first_share = reduce_norm(flat, partial_value, norm_self)
    cross_queries = (
        jnp.dot(first_full, cross_query, preferred_element_type=jnp.float32) * scaling
    ).astype(jnp.bfloat16)
    cross_grid = cross_queries.reshape(steps, requests, local_heads, HEAD_DIM)
    order_rows = (request_order[:, None] == request_ids[None, :]).astype(jnp.bfloat16)
    request_query = jnp.einsum(
        "br,sbhd->srhd", order_rows, cross_grid, preferred_element_type=jnp.float32
    ).astype(jnp.bfloat16)
    enc_local = cross_cache.shape[2]
    enc_keys = cross_cache[:, 0].reshape(requests, enc_local, local_heads, HEAD_DIM)
    enc_values = cross_cache[:, 1].reshape(requests, enc_local, local_heads, HEAD_DIM)
    enc_positions = seq_index * enc_local + jnp.arange(enc_local, dtype=jnp.int32)
    enc_valid = (enc_positions[None, :] < encoder_lengths[:, None])[None, :, None, :]
    enc_scores = jnp.einsum(
        "srhd,rehd->srhe", request_query, enc_keys, preferred_element_type=jnp.float32
    )
    enc_top = global_max(jnp.max(jnp.where(enc_valid, enc_scores, NEG_FILL), axis=3))
    enc_weights = jnp.exp(jnp.where(enc_valid, enc_scores - enc_top[..., None], NEG_FILL))
    enc_numer_local = jnp.einsum(
        "srhe,rehd->srhd",
        enc_weights.astype(jnp.bfloat16),
        enc_values,
        preferred_element_type=jnp.float32,
    )
    enc_denom, enc_numer = global_totals(jnp.sum(enc_weights, axis=3), enc_numer_local)
    enc_attn = (enc_numer / enc_denom[..., None]).astype(jnp.bfloat16)
    cross_attn = jnp.einsum(
        "br,srhd->sbhd", order_rows, enc_attn, preferred_element_type=jnp.float32
    ).astype(jnp.bfloat16)
    partial_value = jnp.dot(
        cross_attn.reshape(steps * requests, local_width),
        cross_output,
        preferred_element_type=jnp.float32,
    )
    second_full, second_share = reduce_norm(first_full, partial_value, norm_cross)
    ffn_hidden = jax.nn.gelu(
        jnp.dot(second_full, feed_up, preferred_element_type=jnp.float32), approximate=False
    ).astype(jnp.bfloat16)
    ignored, out_share = reduce_norm(
        second_full, jnp.dot(ffn_hidden, feed_down, preferred_element_type=jnp.float32), norm_feed
    )
    return out_share.reshape(steps, requests, out_share.shape[1])


def solution(mesh):
    in_specs = (
        P(None, None, "tensor"),
        P(None, "tensor"),
        P(None, "tensor"),
        P(None, "tensor"),
        P("tensor", None),
        P(None, "tensor"),
        P("tensor", None),
        P(None, "tensor"),
        P("tensor", None),
        P(),
        P(),
        P(),
        P("seq", None, None, "tensor"),
        P(None, None, "seq", "tensor"),
        P(),
        P(),
        P(),
        P(),
    )
    out_specs = P(None, None, "tensor")
    return jax.shard_map(
        on_device, mesh=mesh, in_specs=in_specs, out_specs=out_specs, check_vma=False
    )
```

profile of v0, /device:TPU:1, one launch (start us, length us, event | category | flops | bytes accessed | tf_op | source)
XLA Modules:
  0.0 1101.1 jit_solution(13234853274242562757)
XLA Ops:
  7.3 3.9 fusion.134
  11.2 2.6 copy.103
  13.8 2.7 copy.147
  17.8 21.5 %all-gather.2.cloned.1.call-done = bf16[4,128,1024]{2,1,0:T(8,128)(2,1)} async-done(((bf16[4,128,256]{2,1,0:T(8,128)(2,1)}), bf16[4,128,1024]{2,1,0:T(8,128)(2,1)}) %all-gather.2.cloned.1.call-update) | async-done | bytes 1048592 | tf_op jit(solution)/shard_map/all_gather | solution.py:53
  44.4 2.2 convolution_convert_fusion.3
  48.7 3.0 fusion.62
  53.6 128.2 %pmax.14 = f32[4,128,4]{1,2,0:T(4,128)S(1)} all-reduce(f32[4,128,4]{1,2,0:T(4,128)S(1)} %fusion.99), channel_id=1, replica_groups=mesh['seq'=64,'tensor'=4] {'seq'}, use_global_device_ids=true, to_apply=%region_7.8 | all-reduce | flops 2048 | bytes 16384 | tf_op jit(solution)/shard_map/pmax | solution.py:18
  182.7 2.4 convolution_bitcast_fusion.2
  193.8 129.3 %psum.50 = f32[4,128,4]{1,2,0:T(4,128)S(1)} all-reduce(f32[4,128,4]{1,2,0:T(4,128)S(1)} %convolution_bitcast_fusion.4), channel_id=1, replica_groups=mesh['seq'=64,'tensor'=4] {'seq'}, use_global_device_ids=true, to_apply=%region_10.11 | all-reduce | flops 2048 | bytes 16384 | tf_op jit(solution)/shard_map/psum | solution.py:22
  323.1 44.2 %all-reduce.6.cloned.1.call-done = f32[4,128,4,64]{1,3,2,0:T(8,128)} async-done(((f32[4,128,4,64]{1,3,2,0:T(8,128)}), f32[4,128,4,64]{1,3,2,0:T(8,128)}) %all-reduce.6.cloned.1.call-update) | async-done | bytes 524304 | tf_op jit(solution)/shard_map/psum | solution.py:22
  374.2 3.5 copy.129
  377.7 2.2 copy.149
  379.9 3.4 copy.131
  383.4 50.2 %all-reduce.8.cloned.1.call-done = f32[512,1024]{1,0:T(8,128)} async-done(((f32[512,1024]{1,0:T(8,128)}), f32[512,1024]{1,0:T(8,128)}) %all-reduce.8.cloned.1.call-update) | async-done | bytes 2097168 | tf_op jit(solution)/shard_map/psum | solution.py:27
  433.6 2.2 fusion.48
  441.2 4.0 select_reduce_fusion
  445.1 246.6 %pmax.15 = f32[4,128,4]{0,2,1:T(4,128)S(1)} all-reduce(f32[4,128,4]{0,2,1:T(4,128)} %get-tuple-element.30), channel_id=1, replica_groups=mesh['seq'=64,'tensor'=4] {'seq'}, use_global_device_ids=true, to_apply=%region_16.17 | all-reduce | flops 2048 | bytes 16384 | tf_op jit(solution)/shard_map/pmax | solution.py:18
  691.8 3.4 fusion.52
  695.2 2.4 copy.132
  697.7 3.1 fusion.50
  700.8 246.8 %psum.53 = f32[4,128,4]{0,2,1:T(4,128)S(1)} all-reduce(f32[4,128,4]{0,2,1:T(4,128)} %fusion.50), channel_id=1, replica_groups=mesh['seq'=64,'tensor'=4] {'seq'}, use_global_device_ids=true, to_apply=%region_19.20 | all-reduce | flops 2048 | bytes 16384 | tf_op jit(solution)/shard_map/psum | solution.py:22
  951.4 63.0 %all-reduce.12.cloned.1.call-done = f32[512,1024]{1,0:T(8,128)} async-done(((f32[512,1024]{1,0:T(8,128)}), f32[512,1024]{1,0:T(8,128)}) %all-reduce.12.cloned.1.call-update) | async-done | bytes 2097168 | tf_op jit(solution)/shard_map/psum | solution.py:27
  1018.1 9.5 fusion.16
  1028.5 62.9 %all-reduce.14.cloned.1.call-done = f32[512,1024]{1,0:T(8,128)} async-done(((f32[512,1024]{1,0:T(8,128)}), f32[512,1024]{1,0:T(8,128)}) %all-reduce.14.cloned.1.call-update) | async-done | bytes 2097168 | tf_op jit(solution)/shard_map/psum | solution.py:27
  (104 shorter events, 44.2 us)
Async XLA Ops:
  6.5 1011.5 %copy-start = (bf16[1024,1024]{1,0:T(8,128)(2,1)S(1)}, bf16[1024,1024]{1,0:T(8,128)(2,1)}, u32[]{:S(2)}) copy-start(bf16[1024,1024]{1,0:T(8,128)(2,1)} %param.26) | copy-start | bytes 6291460
  6.5 32.7 %all-gather.2.cloned.1.call-start = ((), (), s32[]{:S(2)}) async-start(), calls=%async_computation | async-start | bytes 1310720 | tf_op jit(solution)/shard_map/all_gather | solution.py:53
  7.3 360.1 %all-reduce.6.cloned.1.call-start = ((), (), s32[]{:S(2)}) async-start(), calls=%async_computation.1 | async-start | bytes 1048576 | tf_op jit(solution)/shard_map/psum | solution.py:22
  13.8 2.7 copy-start.9
  13.8 3.3 copy-start.16
  13.8 3.9 copy-start.10
  13.8 25.4 %copy-start.14 = (bf16[1024,256]{1,0:T(8,128)(2,1)S(1)}, bf16[1024,256]{1,0:T(8,128)(2,1)}, u32[]{:S(2)}) copy-start(bf16[1024,256]{1,0:T(8,128)(2,1)} %param.19) | copy-start | bytes 1572868
  40.9 3.5 copy-start.3
  186.6 247.0 %all-reduce.8.cloned.1.call-start = ((), (), s32[]{:S(2)}) async-start(), calls=%async_computation.2 | async-start | bytes 4194304 | tf_op jit(solution)/shard_map/psum | solution.py:27
  193.7 175.1 %copy-start.7 = (bf16[256,1024]{1,0:T(8,128)(2,1)S(1)}, bf16[256,1024]{1,0:T(8,128)(2,1)}, u32[]{:S(2)}) copy-start(bf16[256,1024]{1,0:T(8,128)(2,1)} %param.22) | copy-start | bytes 1572868
  370.7 577.0 %all-reduce.10.cloned.1.call-start = ((), (), s32[]{:S(2)}) async-start(), calls=%async_computation.3 | async-start | bytes 1048576 | tf_op jit(solution)/shard_map/psum | solution.py:22
  374.2 9.1 copy-start.13
  374.2 59.4 %copy-start.4 = (bf16[4,128,1024]{2,1,0:T(8,128)(2,1)S(1)}, bf16[4,128,1024]{2,1,0:T(8,128)(2,1)}, u32[]{:S(2)}) copy-start(bf16[4,128,1024]{2,1,0:T(8,128)(2,1)} %all-gather.2.cloned.1.call-done) | copy-start | bytes 3145732
  379.9 55.9 %copy-start.11 = (f32[1024]{0:T(1024)S(1)}, f32[1024]{0:T(1024)}, u32[]{:S(2)}) copy-start(f32[1024]{0:T(1024)} %param.27) | copy-start | bytes 12292
  433.6 2.2 copy-start.1
  433.6 2.5 copy-start.5
  436.1 1.0 copy-start.15
  697.6 316.8 %all-reduce.12.cloned.1.call-start = ((), (), s32[]{:S(2)}) async-start(), calls=%async_computation.4 | async-start | bytes 4194304 | tf_op jit(solution)/shard_map/psum | solution.py:27
  947.7 1.7 copy-start.8
  951.1 65.5 %copy-start.12 = (f32[1024]{0:T(1024)S(1)}, f32[1024]{0:T(1024)}, u32[]{:S(2)}) copy-start(f32[1024]{0:T(1024)} %param.28) | copy-start | bytes 12292
  951.1 140.2 %all-reduce.14.cloned.1.call-start = ((), (), s32[]{:S(2)}) async-start(), calls=%async_computation.5 | async-start | bytes 4194304 | tf_op jit(solution)/shard_map/psum | solution.py:27
  1014.4 2.2 copy-start.2
  1027.6 63.7 %copy-start.6 = (bf16[512,1024]{1,0:T(8,128)(2,1)S(1)}, bf16[512,1024]{1,0:T(8,128)(2,1)}, u32[]{:S(2)}) copy-start(bf16[512,1024]{1,0:T(8,128)(2,1)} %multiply_convert_fusion) | copy-start | bytes 3145732
Sparse Core Ops, SparseCore 0:
  9.1 30.0 all-gather.1
  186.7 180.5 all-reduce.5
  370.8 62.7 all-reduce.7
  697.7 181.0 all-reduce.9
  951.2 63.1 all-reduce.11
  1027.8 63.5 all-reduce.13
where the time goes:
time: 1100 us
  blocking collectives  751 us (68%)
  waiting for transfers between devices  243 us (22%)
  matrix products  40.3 us (4%)
  local copies, waits for them, and re-layouts  37.1 us (3%)
  other arithmetic  15.7 us (1%)
  between operations  13.8 us (1%)
    psum x2, blocking collectives, global_totals(): return lax.psum((denom, numer), 'seq')  376 us
    pmax x2, blocking collectives, global_max(): return lax.pmax(local_max, 'seq')  375 us
    psum x3, waiting for transfers between devices, reduce_norm(): total = lax.psum(partial_value, 'tensor')  176 us
    psum x2, waiting for transfers between devices, global_totals(): return lax.psum((denom, numer), 'seq')  44.2 us
  transfers between devices with their start and end apart: 6, of which 5 were waited for; matrix products, arithmetic and copies ran while one was open for 3% of the time, Pallas kernels for 0%

commit v1 on v0

--- a/solution.py
+++ b/solution.py
@@ -24,7 +24,9 @@
 
 def reduce_norm(residual, partial_value, gain):
     width = residual.shape[1]
-    total = lax.psum(partial_value, "tensor")
+    total = partial_value
+    for hop in (1, 2):
+        total = total + lax.ppermute(total, "tensor", [(dev, dev ^ hop) for dev in range(4)])
     full = layer_norm(residual.astype(jnp.float32) + total, gain).astype(jnp.bfloat16)
     columns = width // lax.axis_size("tensor")
     return (full, lax.dynamic_slice_in_dim(full, lax.axis_index("tensor") * columns, columns, 1))

time: 1100 us -> 1200 us (1.091); the launches traced: 1100 us -> 1180 us
  waiting for transfers between devices: 243 us -> 310 us
    ppermute x0 -> x6, waiting for transfers between devices: none -> 244 us  [reduce_norm(): lax.ppermute(total, 'tensor', [(dev, dev ^ hop) for dev in range(4)])]
    psum x3 -> x0, waiting for transfers between devices: 176 us -> none  [reduce_norm(): total = lax.psum(partial_value, 'tensor')]
  transfers between devices with their start and end apart: 6 -> 9, of which waited for: 5 -> 8; matrix products, arithmetic and copies ran while one was open for 3% -> 3% of each run, Pallas kernels for 0% -> 0%
where the time goes in v1:
time: 1200 us; the launch traced here: 1180 us
  blocking collectives  755 us (63%)
  waiting for transfers between devices  310 us (26%)
  matrix products  37.3 us (3%)
  local copies, waits for them, and re-layouts  35.7 us (3%)
  other arithmetic  19.5 us (2%)
  between operations  13.5 us (1%)
    pmax x2, blocking collectives, global_max(): return lax.pmax(local_max, 'seq')  380 us
    psum x2, blocking collectives, global_totals(): return lax.psum((denom, numer), 'seq')  376 us
    ppermute x6, waiting for transfers between devices, reduce_norm(): lax.ppermute(total, 'tensor', [(dev, dev ^ hop) for dev in range(4)])  244 us
    psum x2, waiting for transfers between devices, global_totals(): return lax.psum((denom, numer), 'seq')  44.1 us
  transfers between devices with their start and end apart: 9, of which 8 were waited for; matrix products, arithmetic and copies ran while one was open for 3% of the time, Pallas kernels for 0%

profile of v1, /device:TPU:1, one launch (start us, length us, event | category | flops | bytes accessed | tf_op | source)
XLA Modules:
  0.0 1179.3 jit_solution(15082837149224939632)
XLA Ops:
  7.3 3.9 fusion.135
  11.2 2.6 copy.103
  13.8 2.7 copy.147
  17.8 21.5 %all-gather.2.cloned.1.call-done = bf16[4,128,1024]{2,1,0:T(8,128)(2,1)} async-done(((bf16[4,128,256]{2,1,0:T(8,128)(2,1)}), bf16[4,128,1024]{2,1,0:T(8,128)(2,1)}) %all-gather.2.cloned.1.call-update) | async-done | bytes 1048592 | tf_op jit(solution)/shard_map/all_gather | solution.py:55
  48.7 3.0 fusion.60
  53.5 128.2 %pmax.14 = f32[4,128,4]{1,2,0:T(4,128)S(1)} all-reduce(f32[4,128,4]{1,2,0:T(4,128)S(1)} %fusion.97), channel_id=1, replica_groups=mesh['seq'=64,'tensor'=4] {'seq'}, use_global_device_ids=true, to_apply=%region_7.8 | all-reduce | flops 2048 | bytes 16384 | tf_op jit(solution)/shard_map/pmax | solution.py:18
  193.8 129.3 %psum.29 = f32[4,128,4]{1,2,0:T(4,128)S(1)} all-reduce(f32[4,128,4]{1,2,0:T(4,128)S(1)} %convolution_bitcast_fusion.4), channel_id=1, replica_groups=mesh['seq'=64,'tensor'=4] {'seq'}, use_global_device_ids=true, to_apply=%region_10.11 | all-reduce | flops 2048 | bytes 16384 | tf_op jit(solution)/shard_map/psum | solution.py:22
  323.1 44.1 %all-reduce.3.cloned.1.call-done = f32[4,128,4,64]{1,3,2,0:T(8,128)} async-done(((f32[4,128,4,64]{1,3,2,0:T(8,128)}), f32[4,128,4,64]{1,3,2,0:T(8,128)}) %all-reduce.3.cloned.1.call-update) | async-done | bytes 524304 | tf_op jit(solution)/shard_map/psum | solution.py:22
  370.5 43.1 %collective-permute-done = f32[512,1024]{1,0:T(8,128)S(1)} collective-permute-done((f32[512,1024]{1,0:T(8,128)S(1)}, f32[512,1024]{1,0:T(8,128)S(1)}, u32[]{:S(2)}, u32[]{:S(2)}) %collective-permute-start) | collective-permute-done | bytes 2097184 | tf_op jit(solution)/shard_map/ppermute | solution.py:29
  415.4 2.7 collective-permute-start.1
  424.5 2.5 copy.131
  427.2 33.4 %collective-permute-done.1 = f32[512,1024]{1,0:T(8,128)} collective-permute-done((f32[512,1024]{1,0:T(8,128)}, f32[512,1024]{1,0:T(8,128)}, u32[]{:S(2)}, u32[]{:S(2)}) %collective-permute-start.1) | collective-permute-done | bytes 2097184 | tf_op jit(solution)/shard_map/ppermute | solution.py:29
  460.6 3.0 fusion.134
  469.0 3.9 select_reduce_fusion
  472.9 251.3 %pmax.15 = f32[4,128,4]{0,2,1:T(4,128)S(1)} all-reduce(f32[4,128,4]{0,2,1:T(4,128)} %get-tuple-element.32), channel_id=1, replica_groups=mesh['seq'=64,'tensor'=4] {'seq'}, use_global_device_ids=true, to_apply=%region_15.16 | all-reduce | flops 2048 | bytes 16384 | tf_op jit(solution)/shard_map/pmax | solution.py:18
  724.2 3.1 fusion.50
  732.2 246.2 %psum.31 = f32[4,128,4]{0,2,1:T(4,128)S(1)} all-reduce(f32[4,128,4]{0,2,1:T(4,128)S(1)} %fusion.48), channel_id=1, replica_groups=mesh['seq'=64,'tensor'=4] {'seq'}, use_global_device_ids=true, to_apply=%region_18.19 | all-reduce | flops 2048 | bytes 16384 | tf_op jit(solution)/shard_map/psum | solution.py:22
  981.9 40.4 %collective-permute-done.2 = f32[512,1024]{1,0:T(8,128)S(1)} collective-permute-done((f32[512,1024]{1,0:T(8,128)S(1)}, f32[512,1024]{1,0:T(8,128)S(1)}, u32[]{:S(2)}, u32[]{:S(2)}) %collective-permute-start.2) | collective-permute-done | bytes 2097184 | tf_op jit(solution)/shard_map/ppermute | solution.py:29
  1022.6 3.0 collective-permute-start.3
  1025.6 44.6 %collective-permute-done.3 = f32[512,1024]{1,0:T(8,128)S(1)} collective-permute-done((f32[512,1024]{1,0:T(8,128)S(1)}, f32[512,1024]{1,0:T(8,128)S(1)}, u32[]{:S(2)}, u32[]{:S(2)}) %collective-permute-start.3) | collective-permute-done | bytes 2097184 | tf_op jit(solution)/shard_map/ppermute | solution.py:29
  1072.2 9.8 fusion.16
  1082.0 41.9 %collective-permute-done.4 = f32[512,1024]{1,0:T(8,128)S(1)} collective-permute-done((f32[512,1024]{1,0:T(8,128)}, f32[512,1024]{1,0:T(8,128)S(1)}, u32[]{:S(2)}, u32[]{:S(2)}) %collective-permute-start.4) | collective-permute-done | bytes 2097184 | tf_op jit(solution)/shard_map/ppermute | solution.py:29
  1127.9 40.2 %collective-permute-done.5 = f32[512,1024]{1,0:T(8,128)} collective-permute-done((f32[512,1024]{1,0:T(8,128)S(1)}, f32[512,1024]{1,0:T(8,128)}, u32[]{:S(2)}, u32[]{:S(2)}) %collective-permute-start.5) | collective-permute-done | bytes 2097184 | tf_op jit(solution)/shard_map/ppermute | solution.py:29
  1168.1 3.7 fusion.132
  (108 shorter events, 57.7 us)
Async XLA Ops:
  6.5 1065.6 %copy-start = (bf16[1024,1024]{1,0:T(8,128)(2,1)S(1)}, bf16[1024,1024]{1,0:T(8,128)(2,1)}, u32[]{:S(2)}) copy-start(bf16[1024,1024]{1,0:T(8,128)(2,1)} %param.26) | copy-start | bytes 6291460
  6.5 32.7 %all-gather.2.cloned.1.call-start = ((), (), s32[]{:S(2)}) async-start(), calls=%async_computation | async-start | bytes 1310720 | tf_op jit(solution)/shard_map/all_gather | solution.py:55
  7.3 360.0 %all-reduce.3.cloned.1.call-start = ((), (), s32[]{:S(2)}) async-start(), calls=%async_computation.1 | async-start | bytes 1048576 | tf_op jit(solution)/shard_map/psum | solution.py:22
  13.8 2.7 copy-start.9
  13.8 3.3 copy-start.16
  13.8 3.9 copy-start.10
  13.8 25.5 %copy-start.14 = (bf16[1024,256]{1,0:T(8,128)(2,1)S(1)}, bf16[1024,256]{1,0:T(8,128)(2,1)}, u32[]{:S(2)}) copy-start(bf16[1024,256]{1,0:T(8,128)(2,1)} %param.19) | copy-start | bytes 1572868
  40.9 3.5 copy-start.5
  186.5 792.0 %all-reduce.5.cloned.1.call-start = ((), (), s32[]{:S(2)}) async-start(), calls=%async_computation.2 | async-start | bytes 1048576 | tf_op jit(solution)/shard_map/psum | solution.py:22
  193.8 175.0 %copy-start.7 = (bf16[256,1024]{1,0:T(8,128)(2,1)S(1)}, bf16[256,1024]{1,0:T(8,128)(2,1)}, u32[]{:S(2)}) copy-start(bf16[256,1024]{1,0:T(8,128)(2,1)} %param.22) | copy-start | bytes 1572868
  369.2 44.4 %collective-permute-start = (f32[512,1024]{1,0:T(8,128)S(1)}, f32[512,1024]{1,0:T(8,128)S(1)}, u32[]{:S(2)}, u32[]{:S(2)}) collective-permute-start(f32[512,1024]{1,0:T(8,128)S(1)} %fusion.69), channel_id=1, source_target_pairs={{0,1},{1,0},{2,3},{3,2},{4,5},{5,4},{6,7},{7,6},{8,9},{9,8},{10,11... | collective-permute-start | bytes 6291464 | tf_op jit(solution)/shard_map/ppermute | solution.py:29
  415.4 45.3 %collective-permute-start.1 = (f32[512,1024]{1,0:T(8,128)}, f32[512,1024]{1,0:T(8,128)}, u32[]{:S(2)}, u32[]{:S(2)}) collective-permute-start(f32[512,1024]{1,0:T(8,128)} %add.131), channel_id=1, source_target_pairs={{0,2},{1,3},{2,0},{3,1},{4,6},{5,7},{6,4},{7,5},{8,10},{9,11},{10,... | collective-permute-start | bytes 6291464 | tf_op jit(solution)/shard_map/ppermute | solution.py:29
  421.6 5.5 copy-start.13
  427.2 37.8 %copy-start.11 = (f32[1024]{0:T(1024)S(1)}, f32[1024]{0:T(1024)}, u32[]{:S(2)}) copy-start(f32[1024]{0:T(1024)} %param.27) | copy-start | bytes 12292
  427.2 37.8 %copy-start.15 = (bf16[1024,256]{1,0:T(8,128)(2,1)S(1)}, bf16[1024,256]{1,0:T(8,128)(2,1)}, u32[]{:S(2)}) copy-start(bf16[1024,256]{1,0:T(8,128)(2,1)} %param.23) | copy-start | bytes 1572868
  466.7 257.5 %copy-start.6 = (bf16[128,8,4,64]{3,1,2,0:T(8,128)(2,1)S(1)}, bf16[128,8,4,64]{3,1,2,0:T(8,128)(2,1)}, u32[]{:S(2)}) copy-start(bf16[128,8,4,64]{3,1,2,0:T(8,128)(2,1)} %copy.131) | copy-start | bytes 1572868
  729.7 250.4 %copy-start.8 = (bf16[256,1024]{1,0:T(8,128)(2,1)S(1)}, bf16[256,1024]{1,0:T(8,128)(2,1)}, u32[]{:S(2)}) copy-start(bf16[256,1024]{1,0:T(8,128)(2,1)} %param.24) | copy-start | bytes 1572868
  980.6 89.7 %copy-start.3 = (f32[512,1024]{1,0:T(8,128)S(1)}, f32[512,1024]{1,0:T(8,128)}, u32[]{:S(2)}) copy-start(f32[512,1024]{1,0:T(8,128)} %copy-done.2) | copy-start | bytes 6291460
  980.6 41.6 %collective-permute-start.2 = (f32[512,1024]{1,0:T(8,128)S(1)}, f32[512,1024]{1,0:T(8,128)S(1)}, u32[]{:S(2)}, u32[]{:S(2)}) collective-permute-start(f32[512,1024]{1,0:T(8,128)S(1)} %fusion.66), channel_id=1, source_target_pairs={{0,1},{1,0},{2,3},{3,2},{4,5},{5,4},{6,7},{7,6},{8,9},{9,8},{10,11... | collective-permute-start | bytes 6291464 | tf_op jit(solution)/shard_map/ppermute | solution.py:29
  1022.6 49.5 %copy-start.12 = (f32[1024]{0:T(1024)S(1)}, f32[1024]{0:T(1024)}, u32[]{:S(2)}) copy-start(f32[1024]{0:T(1024)} %param.28) | copy-start | bytes 12292
  1022.6 47.6 %collective-permute-start.3 = (f32[512,1024]{1,0:T(8,128)S(1)}, f32[512,1024]{1,0:T(8,128)S(1)}, u32[]{:S(2)}, u32[]{:S(2)}) collective-permute-start(f32[512,1024]{1,0:T(8,128)S(1)} %add.137), channel_id=1, source_target_pairs={{0,2},{1,3},{2,0},{3,1},{4,6},{5,7},{6,4},{7,5},{8,10},{9,11},{10,... | collective-permute-start | bytes 6291464 | tf_op jit(solution)/shard_map/ppermute | solution.py:29
  1082.0 41.9 %collective-permute-start.4 = (f32[512,1024]{1,0:T(8,128)}, f32[512,1024]{1,0:T(8,128)S(1)}, u32[]{:S(2)}, u32[]{:S(2)}) collective-permute-start(f32[512,1024]{1,0:T(8,128)} %fusion.16), channel_id=1, source_target_pairs={{0,1},{1,0},{2,3},{3,2},{4,5},{5,4},{6,7},{7,6},{8,9},{9,8},{10,11... | collective-permute-start | bytes 6291464 | tf_op jit(solution)/shard_map/ppermute | solution.py:29
  1127.1 41.0 %collective-permute-start.5 = (f32[512,1024]{1,0:T(8,128)S(1)}, f32[512,1024]{1,0:T(8,128)}, u32[]{:S(2)}, u32[]{:S(2)}) collective-permute-start(f32[512,1024]{1,0:T(8,128)S(1)} %add.141), channel_id=1, source_target_pairs={{0,2},{1,3},{2,0},{3,1},{4,6},{5,7},{6,4},{7,5},{8,10},{9,11},{10,... | collective-permute-start | bytes 6291464 | tf_op jit(solution)/shard_map/ppermute | solution.py:29
  1168.1 4.7 copy-start.1
  (2 other events, 2.6 us)
Sparse Core Ops, SparseCore 0:
  9.1 30.0 all-gather.1
  186.7 180.5 all-reduce.2
  729.8 183.1 all-reduce.4
